TPU v7x, 128 devices: a whole 4x4x4 slice. The times are simulated.
128 devices in a mesh: feat: 32 (over z, x_hi, y), ex: 4 (over x_lo, core).
Axes of the slice: x: 4 (x_hi: 2, x_lo: 2; x = x_hi * 2 + x_lo), y: 4, z: 4, core: 2. Of those that a mesh axis runs over, the one named last changes fastest.
Arguments:
- grads: bfloat16 [256, 4194304], P('ex', 'feat'), may hold values from -6 to 6
- sign_bits: int32 [4194304], P('feat'), may hold values from 0 to 1
- sample_offset: int32 [8192], replicated, may hold values from 0 to 511
- queries: bfloat16 [16384, 8192], P('ex', 'feat'), may hold values from -6 to 6
- panel_order: int32 [32], replicated, may hold values from 0 to 31, each once
Outputs:
- scores: float32 [256, 16384], P('ex', 'feat')
Inputs may be any that keep to these rules, and one draw needn't show every extreme that they name: sample_offset is below 512. panel_order is a permutation.
All inputs are finite; a program needn't handle non-finite values.
Results may differ from a plain program's by a relative error of at most 0.018.
Values may be sent and summed in bfloat16 or wider, within the bound.
No kernel may reach another device: no remote copies, remote signals or barrier semaphores. Data moves between devices by JAX's collectives and lax.ppermute only.
A program may use at most 192 MiB of HBM per device.

v0:
```python
import math
import jax
import jax.numpy as jnp
from jax import lax
from jax.sharding import PartitionSpec as P

HA = 256
HB = 512
PROJ = 8192


def parity_of(values, bits):
    total = jnp.zeros_like(values)
    for position in range(bits):
        total = total ^ values >> position & 1
    return total


def hadamard_table(order, scale, dtype):
    index = jnp.arange(order, dtype=jnp.int32)
    parity = parity_of(index[:, None] & index[None, :], order.bit_length() - 1)
    return ((1 - 2 * parity).astype(jnp.float32) * scale).astype(dtype)


def hadamard_rows(index, order, scale):
    column = jnp.arange(order, dtype=jnp.int32)
    parity = parity_fold(index[..., None] & column, order.bit_length() - 1)
    return ((1 - 2 * parity).astype(jnp.float32) * scale).astype(jnp.bfloat16)


def parity_fold(values, bits):
    shift = 1
    while shift < bits:
        shift *= 2
    while shift >= 1:
        values = values ^ values >> shift
        shift //= 2
    return values & 1


def power_scale(order):
    return 0.5 ** ((order.bit_length() - 1) // 2)


def on_device(grads, sign_bits, sample_offset, queries, panel_order):
    shards = lax.axis_size("feat")
    examples, feat_dev = grads.shape
    proj_dev = PROJ // shards
    scale_b = power_scale(HB)
    scale_a = power_scale(HA)
    cross = power_scale(feat_dev * shards) / (scale_a * scale_b)
    device_id = lax.axis_index("feat")
    signed = grads * (1 - 2 * sign_bits).astype(jnp.bfloat16)[None, :]
    table_a = hadamard_table(HA, scale_a, jnp.bfloat16)
    turned = jnp.einsum(
        "ca,eab->ceb", table_a, signed.reshape(examples, HA, HB), preferred_element_type=jnp.float32
    )
    rows = hadamard_rows(sample_offset.reshape(shards, proj_dev), HB, scale_b)
    picked = lax.dot_general(
        turned.astype(jnp.bfloat16),
        rows,
        (((2,), (2,)), ((0,), (1,))),
        preferred_element_type=jnp.float32,
    )
    local = picked.astype(jnp.bfloat16)
    full_table = hadamard_table(shards, 1.0, jnp.bfloat16)
    signs = lax.dynamic_slice_in_dim(full_table, device_id, 1, 1)[:, 0]
    outgoing = jnp.transpose(local, (2, 1, 0)) * signs[:, None, None]
    returned = lax.all_to_all(outgoing, "feat", split_axis=0, concat_axis=0, tiled=True)
    projected = (jnp.sum(returned.astype(jnp.float32), axis=0) * cross).astype(jnp.bfloat16)
    every = lax.all_gather(projected, "ex", axis=0, tiled=True)
    ex_count = lax.axis_size("ex")
    panel_count = panel_order.shape[0]
    per_row = panel_count // ex_count
    partial_value = lax.dot_general(
        every.reshape(ex_count, examples, -1),
        queries.reshape(per_row, -1, queries.shape[1]),
        (((2,), (2,)), ((), ())),
        preferred_element_type=jnp.float32,
    )
    partial_value = jnp.transpose(partial_value * (1.0 / math.sqrt(PROJ)), (0, 2, 1, 3))
    partial_value = partial_value.astype(jnp.bfloat16)
    mine = lax.all_to_all(partial_value, "ex", split_axis=0, concat_axis=0, tiled=True)
    ordered = jnp.take(mine.reshape(panel_count, examples, -1), panel_order, axis=0, mode="clip")
    gathered = lax.all_to_all(ordered, "feat", split_axis=0, concat_axis=0, tiled=True)
    return jnp.sum(gathered.astype(jnp.float32), axis=0)


def solution(mesh):
    in_specs = (P("ex", "feat"), P("feat"), P(), P("ex", "feat"), P())
    out_specs = P("ex", "feat")
    return jax.shard_map(
        on_device, mesh=mesh, in_specs=in_specs, out_specs=out_specs, check_vma=False
    )
```

profile of v0, /device:TPU:8, one launch (start us, length us, event | category | flops | bytes accessed | tf_op | source)
XLA Modules:
  0.0 161.5 jit_solution(10771877939283327149)
XLA Ops:
  0.0 0.0 copy-start
  0.0 1.2 subtract_convert_fusion
  1.3 8.5 %broadcast_multiply_fusion = bf16[64,131072]{1,0:T(8,128)(2,1)S(1)} fusion(bf16[64,131072]{1,0:T(8,128)(2,1)} %param.5, bf16[131072]{0:T(1024)(128)(2,1)S(1)} %subtract_convert_fusion), kind=kLoop, calls=%fused_computation.22 | loop fusion | flops 8388608 | bytes 33816576 | tf_op jit(solution)/shard_map/mul | solution.py:53
  9.8 8.8 %copy.24 = bf16[8,8,256,512]{3,2,1,0:T(8,128)(2,1)} copy(bf16[8,8,256,512]{3,1,2,0:T(8,128)(2,1)S(1)} %bitcast.25) | data formatting | bytes 33554432
  18.6 0.0 copy-start.1
  18.6 14.0 %convolution_convert_fusion = bf16[256,64,512]{2,0,1:T(8,128)(2,1)} fusion(bf16[64,256,512]{2,1,0:T(8,128)(2,1)} %bitcast.24), kind=kOutput, calls=%fused_computation.14 | convolution fusion | flops 4305256448 | bytes 33554432 | tf_op jit(solution)/shard_map/ca,eab->ceb/dot_general | solution.py:55
  32.5 0.0 copy-done.1
  32.6 0.1 copy.17
  32.7 0.0 copy-start.2
  32.7 20.6 %multiply_bitcast_fusion = bf16[32,64,256]{1,0,2:T(8,128)(2,1)} fusion(s32[32,256]{0,1:T(8,128)S(1)} %copy.17, bf16[256,64,512]{2,0,1:T(8,128)(2,1)} %convolution_convert_fusion, bf16[32]{0:T(256)(128)(2,1)S(1)} %convert_bitcast_fusion), kind=kOutput, calls=%fused_computation.26 | convolution fusion | flops 609222656 | bytes 17858624 | tf_op jit(solution)/shard_map/dot_general | solution.py:59
  53.3 2.8 %copy.19 = bf16[32,64,256]{2,1,0:T(8,128)(2,1)S(1)} copy(bf16[32,64,256]{1,0,2:T(8,128)(2,1)} %multiply_bitcast_fusion) | data formatting | bytes 2097152 | tf_op jit(solution)/shard_map/mul | solution.py:68
  56.1 28.7 %all_to_all.15 = bf16[32,64,256]{2,1,0:T(8,128)(2,1)S(1)} all-to-all(bf16[32,64,256]{2,1,0:T(8,128)(2,1)S(1)} %copy.19), channel_id=1, replica_groups=mesh['feat'=32,'ex'=4] {'feat'}, dimensions={0} | all-to-all | bytes 2097152 | tf_op jit(solution)/shard_map/all_to_all | solution.py:69
  84.8 0.2 convert_reduce_fusion.1
  84.9 5.4 %all_gather.3 = bf16[256,256]{1,0:T(8,128)(2,1)S(1)} all-gather(bf16[64,256]{1,0:T(8,128)(2,1)S(1)} %multiply_convert_fusion.2), channel_id=1, replica_groups=mesh['feat'=32,'ex'=4] {'ex'}, dimensions={0}, use_global_device_ids=true | all-gather | bytes 163840 | tf_op jit(solution)/shard_map/all_gather | solution.py:71
  90.4 0.0 copy-done
  90.4 2.1 %fusion.20 = bf16[4,8,64,512]{3,2,1,0:T(8,128)(2,1)} fusion(bf16[4,64,256,1]{2,1,3,0:T(8,128)(2,1)S(1)} %bitcast.26, bf16[8,512,256,1]{2,1,0,3:T(8,128)(2,1)S(1)} %bitcast.23), kind=kOutput, calls=%fused_computation.27 | convolution fusion | flops 538968064 | bytes 4325376 | tf_op jit(solution)/shard_map/dot_general | solution.py:75
  92.4 4.4 %all-to-all-start.1 = ((bf16[4,8,64,512]{3,2,1,0:T(8,128)(2,1)}), bf16[4,8,64,512]{3,2,1,0:T(8,128)(2,1)}, u32[]{:S(2)}, u32[]{:S(2)}) async-start(bf16[4,8,64,512]{3,2,1,0:T(8,128)(2,1)} %fusion.20), calls=%async_computation.1 | async-start | bytes 4194304 | tf_op jit(solution)/shard_map/all_to_all | solution.py:83
  96.8 0.0 copy-done.2
  96.9 25.7 %all-to-all-done.1 = bf16[4,8,64,512]{3,2,1,0:T(8,128)(2,1)} async-done(((bf16[4,8,64,512]{3,2,1,0:T(8,128)(2,1)}), bf16[4,8,64,512]{3,2,1,0:T(8,128)(2,1)}, u32[]{:S(2)}, u32[]{:S(2)}) %all-to-all-start.1) | async-done | bytes 2097184 | tf_op jit(solution)/shard_map/all_to_all | solution.py:83
  122.6 3.6 %gather_fusion = bf16[32,64,512]{2,1,0:T(8,128)(2,1)} fusion(bf16[32,64,512]{2,1,0:T(8,128)(2,1)} %bitcast.9, s32[1024]{0:T(1024)S(1)} %pad_clamp_fusion), kind=kCustom, calls=%fused_computation | custom fusion | bytes 4194432 | tf_op jit(solution)/shard_map/jit(_take)/gather | solution.py:84
  126.2 34.4 %all_to_all.16 = bf16[32,64,512]{2,1,0:T(8,128)(2,1)S(1)} all-to-all(bf16[32,64,512]{2,1,0:T(8,128)(2,1)} %gather_fusion), channel_id=1, replica_groups=mesh['feat'=32,'ex'=4] {'feat'}, dimensions={0} | all-to-all | bytes 4194304 | tf_op jit(solution)/shard_map/all_to_all | solution.py:85
  160.5 0.9 convert_reduce_fusion
  (6 shorter events, 0.1 us)
Async XLA Ops:
  0.0 90.4 %copy-start = (bf16[4096,256]{1,0:T(8,128)(2,1)S(1)}, bf16[4096,256]{1,0:T(8,128)(2,1)}, u32[]{:S(2)}) copy-start(bf16[4096,256]{1,0:T(8,128)(2,1)} %param.8) | copy-start | bytes 6291460
  18.6 14.0 %copy-start.1 = (s32[8192]{0:T(1024)S(1)}, s32[8192]{0:T(1024)}, u32[]{:S(2)}) copy-start(s32[8192]{0:T(1024)} %param.7) | copy-start | bytes 98308
  32.7 64.2 %copy-start.2 = (s32[32]{0:T(128)S(1)}, s32[32]{0:T(128)}, u32[]{:S(2)}) copy-start(s32[32]{0:T(128)} %param.9) | copy-start | bytes 388
  92.4 30.2 %all-to-all-start.1 = ((bf16[4,8,64,512]{3,2,1,0:T(8,128)(2,1)}), bf16[4,8,64,512]{3,2,1,0:T(8,128)(2,1)}, u32[]{:S(2)}, u32[]{:S(2)}) async-start(bf16[4,8,64,512]{3,2,1,0:T(8,128)(2,1)} %fusion.20), calls=%async_computation.1 | async-start | bytes 4194304 | tf_op jit(solution)/shard_map/all_to_all | solution.py:83
where the time goes:
time: 162 us; the launch traced here: 161 us
  blocking collectives  68.5 us (42%)
  matrix products  36.6 us (23%)
  waiting for transfers between devices  25.7 us (16%)
  local copies, waits for them, and re-layouts  15.3 us (9%)
  other arithmetic  10.9 us (7%)
  starting transfers between devices  4.43 us (3%)
    all_to_all x1, blocking collectives, on_device(): lax.all_to_all(ordered, 'feat', split_axis=0, concat_axis=0, tiled=True)  34.4 us
    all_to_all x1, blocking collectives, on_device(): lax.all_to_all(outgoing, 'feat', split_axis=0, concat_axis=0, tiled=True)  28.7 us
    all_to_all x1, waiting for transfers between devices, on_device(): lax.all_to_all(partial_value, 'ex', split_axis=0, concat_axis=0, tiled=True)  25.7 us
    dot_general x1, matrix products, on_device(): lax.dot_general(turned.astype(jnp.bfloat16), rows, (((2,), (2,)), ((0,),...  20.6 us
    dot_general x1, matrix products, on_device(): jnp.einsum('ca,eab->ceb', table_a, signed.reshape(examples, HA, HB), pref...  14 us
    unnamed x7, local copies, waits for them, and re-layouts  8.79 us
    mul x1, other arithmetic, on_device(): signed = grads * (1 - 2 * sign_bits).astype(jnp.bfloat16)[None, :]  8.52 us
    all_gather x1, blocking collectives, on_device(): every = lax.all_gather(projected, 'ex', axis=0, tiled=True)  5.42 us
  transfers between devices with their start and end apart: 1, of which 1 were waited for; matrix products, arithmetic and copies ran while one was open for 0% of the time, Pallas kernels for 0%

commit v1 on v0

--- a/solution.py
+++ b/solution.py
@@ -68,7 +68,10 @@
     outgoing = jnp.transpose(local, (2, 1, 0)) * signs[:, None, None]
     returned = lax.all_to_all(outgoing, "feat", split_axis=0, concat_axis=0, tiled=True)
     projected = (jnp.sum(returned.astype(jnp.float32), axis=0) * cross).astype(jnp.bfloat16)
-    every = lax.all_gather(projected, "ex", axis=0, tiled=True)
+    _post_fields = lambda x_in, axis_tag: jnp.concatenate(
+        lax.all_to_all(jnp.stack([x_in for _ in range(lax.axis_size(axis_tag))]), axis_tag, 0, 0), 0
+    )
+    every = _post_fields(projected, "ex")
     ex_count = lax.axis_size("ex")
     panel_count = panel_order.shape[0]
     per_row = panel_count // ex_count

time: 162 us -> 180 us (1.11)
  other arithmetic: 10.9 us -> 21.6 us
  matrix products: 36.6 us -> 42.1 us
    convert_element_type x0 -> x1, other arithmetic: none -> 10.6 us  [hadamard_rows(): return ((1 - 2 * parity).astype(jnp.float32) * scale).astype(jnp.bfloat16)]
    all_to_all x0 -> x1, blocking collectives: none -> 6.99 us  [on_device(): lax.all_to_all(jnp.stack([x_in for _ in range(lax.axis_size(axis_tag))]),...]
    dot_general x1, matrix products: 20.6 us -> 26.1 us  [on_device(): lax.dot_general(turned.astype(jnp.bfloat16), rows, (((2,), (2,)), ((0,),...]
    all_gather x1 -> x0, blocking collectives: 5.42 us -> none  [on_device(): every = lax.all_gather(projected, 'ex', axis=0, tiled=True)]
    dot_general x0 -> x1, local copies, waits for them, and re-layouts: none -> 2.8 us  [on_device(): lax.dot_general(turned.astype(jnp.bfloat16), rows, (((2,), (2,)), ((0,),...]
    mul x1 -> x0, local copies, waits for them, and re-layouts: 2.79 us -> none  [on_device(): outgoing = jnp.transpose(local, (2, 1, 0)) * signs[:, None, None]]
where the time goes in v1:
time: 180 us; the launch traced here: 179 us
  blocking collectives  70 us (39%)
  matrix products  42.1 us (23%)
  waiting for transfers between devices  25.7 us (14%)
  other arithmetic  21.6 us (12%)
  local copies, waits for them, and re-layouts  15.2 us (8%)
  starting transfers between devices  4.43 us (2%)
    all_to_all x1, blocking collectives, on_device(): lax.all_to_all(ordered, 'feat', split_axis=0, concat_axis=0, tiled=True)  34.4 us
    all_to_all x1, blocking collectives, on_device(): lax.all_to_all(outgoing, 'feat', split_axis=0, concat_axis=0, tiled=True)  28.7 us
    dot_general x1, matrix products, on_device(): lax.dot_general(turned.astype(jnp.bfloat16), rows, (((2,), (2,)), ((0,),...  26.1 us
    all_to_all x1, waiting for transfers between devices, on_device(): lax.all_to_all(partial_value, 'ex', split_axis=0, concat_axis=0, tiled=True)  25.7 us
    dot_general x1, matrix products, on_device(): jnp.einsum('ca,eab->ceb', table_a, signed.reshape(examples, HA, HB), pref...  13.9 us
    convert_element_type x1, other arithmetic, hadamard_rows(): return ((1 - 2 * parity).astype(jnp.float32) * scale).astype(jnp.bfloat16)  10.6 us
    unnamed x7, local copies, waits for them, and re-layouts  8.78 us
    mul x1, other arithmetic, on_device(): signed = grads * (1 - 2 * sign_bits).astype(jnp.bfloat16)[None, :]  8.52 us
  transfers between devices with their start and end apart: 1, of which 1 were waited for; matrix products, arithmetic and copies ran while one was open for 0% of the time, Pallas kernels for 0%

profile of v1, /device:TPU:8, one launch (start us, length us, event | category | flops | bytes accessed | tf_op | source)
XLA Modules:
  0.0 179.2 jit_solution(16965702583146081858)
XLA Ops:
  0.0 0.0 copy-start
  0.0 1.2 subtract_convert_fusion
  1.3 8.5 %broadcast_multiply_fusion = bf16[64,131072]{1,0:T(8,128)(2,1)S(1)} fusion(bf16[64,131072]{1,0:T(8,128)(2,1)} %param.5, bf16[131072]{0:T(1024)(128)(2,1)S(1)} %subtract_convert_fusion), kind=kLoop, calls=%fused_computation.15 | loop fusion | flops 8388608 | bytes 33816576 | tf_op jit(solution)/shard_map/mul | solution.py:53
  9.8 8.8 %copy.10 = bf16[8,8,256,512]{3,2,1,0:T(8,128)(2,1)} copy(bf16[8,8,256,512]{3,1,2,0:T(8,128)(2,1)S(1)} %bitcast.24) | data formatting | bytes 33554432
  18.6 0.0 copy-start.1
  18.6 13.9 %fusion.10 = bf16[256,64,512]{2,0,1:T(8,128)(2,1)} fusion(bf16[64,256,512]{2,1,0:T(8,128)(2,1)} %bitcast.23), kind=kOutput, calls=%fused_computation.24 | convolution fusion | flops 4296867840 | bytes 33554432 | tf_op jit(solution)/shard_map/ca,eab->ceb/dot_general | solution.py:55
  32.5 0.0 copy-done.1
  32.5 10.6 %fusion.6 = bf16[32,256,512]{2,1,0:T(8,128)(2,1)} fusion(s32[32,256]{1,0:T(8,128)S(1)} %and.95), kind=kLoop, calls=%fused_computation.13 | loop fusion | flops 71303168 | bytes 8421376 | tf_op jit(solution)/shard_map/convert_element_type | solution.py:28
  43.1 26.1 %fusion.5 = bf16[256,64,32]{1,2,0:T(8,128)(2,1)} fusion(bf16[256,64,512]{2,0,1:T(8,128)(2,1)} %fusion.10, bf16[32,256,512]{2,1,0:T(8,128)(2,1)} %fusion.6), kind=kOutput, calls=%fused_computation.12 | convolution fusion | flops 536870912 | bytes 26214400 | tf_op jit(solution)/shard_map/dot_general | solution.py:59
  69.3 0.0 copy-start.2
  69.3 2.8 %copy.8 = bf16[256,64,32]{0,1,2:T(8,128)(2,1)S(1)} copy(bf16[256,64,32]{1,2,0:T(8,128)(2,1)} %fusion.5) | data formatting | bytes 2097152 | tf_op jit(solution)/shard_map/dot_general | solution.py:59
  72.1 0.1 multiply_bitcast_fusion
  72.2 28.7 %all_to_all.20 = bf16[32,64,256]{2,1,0:T(8,128)(2,1)S(1)} all-to-all(bf16[32,64,256]{2,1,0:T(8,128)(2,1)S(1)} %multiply_bitcast_fusion), channel_id=1, replica_groups=mesh['feat'=32,'ex'=4] {'feat'}, dimensions={0} | all-to-all | bytes 2097152 | tf_op jit(solution)/shard_map/all_to_all | solution.py:69
  100.9 0.2 convert_reduce_fusion.1
  101.1 7.0 %all_to_all.21 = bf16[4,64,256]{2,1,0:T(8,128)(2,1)S(1)} all-to-all(bf16[4,64,256]{2,1,0:T(8,128)(2,1)S(1)} %stack.2), channel_id=1, replica_groups=mesh['feat'=32,'ex'=4] {'ex'}, dimensions={0} | all-to-all | bytes 262144 | tf_op jit(solution)/shard_map/all_to_all | solution.py:72
  108.1 0.0 copy-done
  108.1 2.1 %fusion.8 = bf16[4,8,64,512]{3,2,1,0:T(8,128)(2,1)} fusion(bf16[8,512,256,1]{2,1,0,3:T(8,128)(2,1)S(1)} %bitcast.22, bf16[4,64,256]{2,1,0:T(8,128)(2,1)S(1)} %all_to_all.21), kind=kOutput, calls=%fused_computation.19 | convolution fusion | flops 538968064 | bytes 4325376 | tf_op jit(solution)/shard_map/dot_general | solution.py:78
  110.1 4.4 %all-to-all-start.2 = ((bf16[4,8,64,512]{3,2,1,0:T(8,128)(2,1)}), bf16[4,8,64,512]{3,2,1,0:T(8,128)(2,1)}, u32[]{:S(2)}, u32[]{:S(2)}) async-start(bf16[4,8,64,512]{3,2,1,0:T(8,128)(2,1)} %fusion.8), calls=%async_computation.2 | async-start | bytes 4194304 | tf_op jit(solution)/shard_map/all_to_all | solution.py:86
  114.6 0.0 copy-done.2
  114.6 25.7 %all-to-all-done.2 = bf16[4,8,64,512]{3,2,1,0:T(8,128)(2,1)} async-done(((bf16[4,8,64,512]{3,2,1,0:T(8,128)(2,1)}), bf16[4,8,64,512]{3,2,1,0:T(8,128)(2,1)}, u32[]{:S(2)}, u32[]{:S(2)}) %all-to-all-start.2) | async-done | bytes 2097184 | tf_op jit(solution)/shard_map/all_to_all | solution.py:86
  140.3 3.6 %gather_fusion = bf16[32,64,512]{2,1,0:T(8,128)(2,1)} fusion(bf16[32,64,512]{2,1,0:T(8,128)(2,1)} %bitcast.8, s32[1024]{0:T(1024)S(1)} %pad_clamp_fusion), kind=kCustom, calls=%fused_computation | custom fusion | bytes 4194432 | tf_op jit(solution)/shard_map/jit(_take)/gather | solution.py:87
  143.9 34.4 %all_to_all.22 = bf16[32,64,512]{2,1,0:T(8,128)(2,1)S(1)} all-to-all(bf16[32,64,512]{2,1,0:T(8,128)(2,1)} %gather_fusion), channel_id=1, replica_groups=mesh['feat'=32,'ex'=4] {'feat'}, dimensions={0} | all-to-all | bytes 4194304 | tf_op jit(solution)/shard_map/all_to_all | solution.py:88
  178.3 0.9 convert_reduce_fusion
  (7 shorter events, 0.1 us)
Async XLA Ops:
  0.0 108.1 %copy-start = (bf16[4096,256]{1,0:T(8,128)(2,1)S(1)}, bf16[4096,256]{1,0:T(8,128)(2,1)}, u32[]{:S(2)}) copy-start(bf16[4096,256]{1,0:T(8,128)(2,1)} %param.8) | copy-start | bytes 6291460
  18.6 14.0 %copy-start.1 = (s32[8192]{0:T(1024)S(1)}, s32[8192]{0:T(1024)}, u32[]{:S(2)}) copy-start(s32[8192]{0:T(1024)} %param.7) | copy-start | bytes 98308
  69.3 45.3 %copy-start.2 = (s32[32]{0:T(128)S(1)}, s32[32]{0:T(128)}, u32[]{:S(2)}) copy-start(s32[32]{0:T(128)} %param.9) | copy-start | bytes 388
  110.1 30.2 %all-to-all-start.2 = ((bf16[4,8,64,512]{3,2,1,0:T(8,128)(2,1)}), bf16[4,8,64,512]{3,2,1,0:T(8,128)(2,1)}, u32[]{:S(2)}, u32[]{:S(2)}) async-start(bf16[4,8,64,512]{3,2,1,0:T(8,128)(2,1)} %fusion.8), calls=%async_computation.2 | async-start | bytes 4194304 | tf_op jit(solution)/shard_map/all_to_all | solution.py:86
